TPU v7x, 32 devices: a whole 2x2x4 slice. The times are simulated.
32 devices in a mesh: seq: 4 (over z), ch: 8 (over y, x, core).
Axes of the slice: x: 2, y: 2, z: 4, core: 2. Of those that a mesh axis runs over, the one named last changes fastest.
Arguments:
- inputs: bfloat16 [1024, 8192], P('seq', 'ch'), may hold values from -6 to 6
- w_in: bfloat16 [3, 8192, 8192], P(None, 'seq', 'ch'), may hold values from -0.0625 to 0.0625
- short_filter: float32 [3, 3, 8192], P(None, None, 'ch'), may hold values from -3 to 3
- rates: float32 [16, 8192], P(None, 'ch'), may hold values from 9.765625e-05 to 0.05
- residues: float32 [16, 8192], P(None, 'ch'), may hold values from -3 to 3
- skip: float32 [8192], P('ch'), may hold values from -3 to 3
Outputs:
- gated: bfloat16 [1024, 8192], P('seq', 'ch')
All inputs are finite; a program needn't handle non-finite values.
Results may differ from a plain program's by a relative error of at most 0.0065.
Values may be sent and summed in bfloat16 or wider, within the bound.
No kernel may reach another device: no remote copies, remote signals or barrier semaphores. Data moves between devices by JAX's collectives and lax.ppermute only.
A program may use at most 128 MiB of HBM per device.

v0:
```python
import jax
import jax.numpy as jnp
from jax import lax
from jax.sharding import PartitionSpec as P

TAPS = 3


def passed_along(block, axis, distance):
    devices = range(lax.axis_size(axis))
    route = [(i - distance, i) for i in devices if i - distance in devices]
    return lax.ppermute(block, axis, route)


def carried_in(part, axis, combine, identity):
    place = lax.axis_index(axis)
    gathered = jax.tree.map(lambda a: lax.all_gather(a, axis), part)
    state = jax.tree.map(lambda a, e: jnp.zeros_like(a) + jnp.asarray(e, a.dtype), part, identity)

    def one(hop, state):
        return combine(
            state, jax.tree.map(lambda a: lax.dynamic_index_in_dim(a, hop, 0, False), gathered)
        )

    return lax.fori_loop(0, place, one, state)


def combine(earlier, later):
    return (earlier[0] * later[0], earlier[1] * later[0] + later[1])


def project(inputs, w_in):
    tok_rows = inputs.shape[0]
    n_seq = lax.axis_size("seq")
    n_ch = lax.axis_size("ch")
    features = lax.all_gather(inputs, "ch", axis=1, tiled=True)
    piece = features.shape[1] // (n_seq * n_ch)
    features = features.reshape(tok_rows, n_seq, n_ch, piece)
    mine = lax.dynamic_index_in_dim(features, lax.axis_index("ch"), 2, False)
    rows = lax.all_to_all(mine, "seq", 1, 0, tiled=True)
    rows = rows.reshape(n_seq * tok_rows, piece)
    block = lax.all_gather(rows, "ch", axis=1, tiled=True)
    partial = jnp.einsum("td,kdc->ktc", block, w_in, preferred_element_type=jnp.float32)
    return lax.psum_scatter(partial, "seq", scatter_dimension=1, tiled=True)


def per_device(inputs, w_in, short_filter, rates, residues, skip):
    tok_rows = inputs.shape[0]
    width = w_in.shape[2]
    modes = rates.shape[0]
    proj = project(inputs, w_in).astype(jnp.bfloat16)
    prior = passed_along(proj[:, tok_rows - (TAPS - 1) :, :], "seq", 1)
    padded = jnp.concatenate([prior, proj], axis=1).astype(jnp.float32)
    mixed = jnp.zeros((3, tok_rows, width), jnp.float32)
    for j in range(TAPS):
        mixed = (
            mixed
            + short_filter[:, j, None, :] * padded[:, TAPS - 1 - j : TAPS - 1 - j + tok_rows, :]
        )
    query, key, value = (mixed[0], mixed[1], mixed[2])
    drive = key * value
    position = jnp.arange(tok_rows, dtype=jnp.float32)
    scaled = residues * jnp.sqrt(1.0 - jnp.exp(-2.0 * rates))
    end_powers = jnp.exp(-rates[None, :, :] * (tok_rows - 1.0 - position)[:, None, None])
    end_state = jnp.sum(end_powers * drive[:, None, :], axis=0)
    block_decay = jnp.exp(-rates * tok_rows)
    identity = (jnp.ones_like(block_decay), jnp.zeros_like(end_state))
    entering = carried_in((block_decay, end_state), "seq", combine, identity)[1]
    start_powers = jnp.exp(-rates[None, :, :] * (position + 1.0)[:, None, None])
    cross = jnp.sum(start_powers * (scaled * entering)[None, :, :], axis=1)
    center = (tok_rows - 1.0) / 2.0
    offset = (position - center)[:, None, None]
    rising = jnp.exp(rates[None, :, :] * offset) * drive[:, None, :]
    offsets = jnp.arange(tok_rows, dtype=jnp.int32)
    lower = (offsets[:, None] >= offsets[None, :]).astype(jnp.float32)
    prefix = jnp.dot(
        lower, rising.reshape(tok_rows, modes * width), precision=lax.Precision.HIGHEST
    )
    prefix = prefix.reshape(tok_rows, modes, width)
    falling = jnp.exp(-rates[None, :, :] * offset) * scaled[None, :, :]
    local = jnp.sum(falling * prefix, axis=1)
    return (query * (local + cross + skip[None, :] * drive)).astype(jnp.bfloat16)


def solution(mesh):
    in_specs = (
        P("seq", "ch"),
        P(None, "seq", "ch"),
        P(None, None, "ch"),
        P(None, "ch"),
        P(None, "ch"),
        P("ch"),
    )
    out_specs = P("seq", "ch")
    return jax.shard_map(
        per_device, mesh=mesh, in_specs=in_specs, out_specs=out_specs, check_vma=False
    )
```

profile of v0, /device:TPU:26, one launch (start us, length us, event | category | flops | bytes accessed | tf_op | source)
XLA Modules:
  0.0 415.0 jit_solution(5616361309072354084)
XLA Ops:
  6.5 0.0 all-gather.5.cloned.1.call-start
  6.5 0.7 all-gather.5.cloned.1.call-update
  7.3 0.0 all-gather.7.cloned.1.call-start
  7.3 39.5 %all-gather.5.cloned.1.call-done = bf16[256,8192]{1,0:T(8,128)(2,1)} async-done(((bf16[256,1024]{1,0:T(8,128)(2,1)}), bf16[256,8192]{1,0:T(8,128)(2,1)}) %all-gather.5.cloned.1.call-update) | async-done | bytes 4194320 | tf_op jit(solution)/shard_map/all_gather | solution.py:36
  46.8 3.6 copy.15
  50.4 1.1 constant_dynamic-slice_fusion
  51.5 0.2 copy.21
  51.7 17.5 %all_to_all.15 = bf16[256,4,256]{2,0,1:T(8,128)(2,1)} all-to-all(bf16[256,4,256]{2,0,1:T(8,128)(2,1)S(1)} %bitcast.60), channel_id=1, replica_groups=mesh['seq'=4,'ch'=8] {'seq'}, dimensions={1} | all-to-all | bytes 1048576 | tf_op jit(solution)/shard_map/all_to_all | solution.py:40
  69.2 0.0 all-gather.7.cloned.1.call-update
  69.2 0.0 reduce-scatter.2.cloned.1.call-start
  69.3 37.4 %all-gather.7.cloned.1.call-done = bf16[1024,2048]{1,0:T(8,128)(2,1)} async-done(((bf16[1024,256]{1,0:T(8,128)(2,1)}), bf16[1024,2048]{1,0:T(8,128)(2,1)}) %all-gather.7.cloned.1.call-update) | async-done | bytes 4194320 | tf_op jit(solution)/shard_map/all_gather | solution.py:42
  106.7 18.9 %convolution_bitcast_fusion = f32[3,1024,1024]{2,1,0:T(8,128)} fusion(bf16[3,2048,1024]{2,1,0:T(8,128)(2,1)} %param.9, bf16[1024,2048]{1,0:T(8,128)(2,1)} %all-gather.7.cloned.1.call-done), kind=kOutput, calls=%fused_computation.6 | convolution fusion | flops 12884901888 | bytes 29360128 | tf_op jit(solution)/shard_map/td,kdc->ktc/dot_general | solution.py:43
  125.6 0.0 copy-start.2
  125.6 0.0 copy-start
  125.6 0.0 reduce-scatter.2.cloned.1.call-update
  125.7 0.7 copy-done.2
  126.5 0.0 copy-done
  126.5 0.6 fusion.9
  127.1 210.6 %reduce-scatter.2.cloned.1.call-done = f32[3,256,1024]{2,1,0:T(8,128)} async-done(((f32[3,1024,1024]{2,1,0:T(8,128)}), f32[3,256,1024]{2,1,0:T(8,128)}) %reduce-scatter.2.cloned.1.call-update) | async-done | bytes 3145744 | tf_op jit(solution)/shard_map/reduce_scatter | solution.py:44
  337.7 2.1 convert_element_type.10
  339.9 1.3 collective-permute-start
  341.2 15.8 %all-gather = f32[64,1024]{1,0:T(8,128)S(1)} all-gather(f32[16,1024]{1,0:T(8,128)S(1)} %get-tuple-element.63), channel_id=2, replica_groups=mesh['seq'=4,'ch'=8] {'seq'}, dimensions={0}, use_global_device_ids=true | all-gather | bytes 327680 | tf_op jit(solution)/shard_map/all_gather | solution.py:17
  357.0 0.6 copy.16
  357.6 0.0 collective-permute-done
  357.6 0.5 maximum_convert_fusion
  358.1 0.9 fusion.1
  359.0 1.2 fusion.3
  360.2 2.5 copy.14
  362.7 4.1 multiply_reduce_fusion.1
  366.8 14.6 %all-gather.1 = f32[64,1024]{1,0:T(8,128)} all-gather(f32[16,1024]{1,0:T(8,128)S(1)} %multiply_reduce_fusion.1), channel_id=3, replica_groups=mesh['seq'=4,'ch'=8] {'seq'}, dimensions={0}, use_global_device_ids=true | all-gather | bytes 327680 | tf_op jit(solution)/shard_map/all_gather | solution.py:17
  381.4 2.9 while.12
  381.4 0.9 bitcast_add_fusion.2
  382.3 0.9 bitcast_add_fusion.2
  383.2 0.9 bitcast_add_fusion.2
  384.3 0.0 copy-start.1
  384.3 0.9 fusion.8
  385.2 3.9 bitcast_multiply_fusion.1
  389.1 0.0 copy-done.1
  389.1 0.0 copy-start.3
  389.2 13.9 %multiply_reduce_fusion.2 = f32[256,1024]{1,0:T(8,128)} fusion(f32[16,1024,256]{2,1,0:T(8,128)S(1)} %bitcast.57, f32[16,1024]{1,0:T(8,128)S(1)} %get-tuple-element.61, f32[256]{0:T(256)S(1)} %iota_add_fusion.1, f32[16,1024]{1,0:T(8,128)S(1)} %copy-done.1), kind=kOutput, calls=%fused_computation.5 | convolution fusion | flops 12901482496 | bytes 17957888 | tf_op jit(solution)/shard_map/dot_general | solution.py:76
  403.1 2.8 multiply_reduce_fusion
  405.9 0.0 copy-done.3
  405.9 2.6 fusion.5
  (8 shorter events, 0.1 us)
Async XLA Ops:
  6.5 40.3 %all-gather.5.cloned.1.call-start = ((), (), s32[]{:S(2)}) async-start(), calls=%async_computation.2 | async-start | bytes 4718592 | tf_op jit(solution)/shard_map/all_gather | solution.py:36
  7.3 99.5 %all-gather.7.cloned.1.call-start = ((), (), s32[]{:S(2)}) async-start(), calls=%async_computation.3 | async-start | bytes 4718592 | tf_op jit(solution)/shard_map/all_gather | solution.py:42
  69.2 268.5 %reduce-scatter.2.cloned.1.call-start = ((), (), s32[]{:S(2)}) async-start(), calls=%async_computation.4 | async-start | bytes 15728640 | tf_op jit(solution)/shard_map/reduce_scatter | solution.py:44
  125.6 0.8 copy-start.2
  125.6 0.9 copy-start
  339.9 17.7 %collective-permute-start = (bf16[3,2,1024]{2,1,0:T(2,128)(2,1)S(1)}, bf16[3,2,1024]{2,1,0:T(2,128)(2,1)S(1)}, u32[]{:S(2)}, u32[]{:S(2)}) collective-permute-start(bf16[3,2,1024]{2,1,0:T(2,128)(2,1)S(1)} %slice.40), channel_id=1, source_target_pairs={{0,8},{8,16},{16,24},{1,9},{9,17},{17,25},{2,10},{10,18},{18,26},{... | collective-permute-start | bytes 36872 | tf_op jit(solution)/shard_map/ppermute | solution.py:12
  384.3 4.8 %copy-start.1 = (f32[16,1024]{1,0:T(8,128)S(1)}, f32[16,1024]{1,0:T(8,128)}, u32[]{:S(2)}) copy-start(f32[16,1024]{1,0:T(8,128)} %get-tuple-element.62) | copy-start | bytes 196612
  389.1 16.7 %copy-start.3 = (f32[1024]{0:T(1024)S(1)}, f32[1024]{0:T(1024)}, u32[]{:S(2)}) copy-start(f32[1024]{0:T(1024)} %param.13) | copy-start | bytes 12292
Sparse Core Ops, SparseCore 0:
  9.2 37.5 all-gather.4
  69.3 37.3 all-gather.6
  125.8 211.8 reduce-scatter.1
where the time goes:
time: 416 us; the launch traced here: 415 us
  waiting for transfers between devices  288 us (69%)
  blocking collectives  47.9 us (12%)
  matrix products  32.8 us (8%)
  other arithmetic  22.3 us (5%)
  between operations  13.3 us (3%)
  local copies, waits for them, and re-layouts  8.82 us (2%)
    reduce_scatter x1, waiting for transfers between devices, project(): return lax.psum_scatter(partial, 'seq', scatter_dimension=1, tiled=True)  211 us
    all_gather x1, waiting for transfers between devices, project(): features = lax.all_gather(inputs, 'ch', axis=1, tiled=True)  39.5 us
    all_gather x1, waiting for transfers between devices, project(): block = lax.all_gather(rows, 'ch', axis=1, tiled=True)  37.4 us
    all_gather x2, blocking collectives, carried_in(): gathered = jax.tree.map(lambda a: lax.all_gather(a, axis), part)  30.4 us
    dot_general x1, matrix products, project(): jnp.einsum('td,kdc->ktc', block, w_in, preferred_element_type=jnp.float32)  18.9 us
    all_to_all x1, blocking collectives, project(): rows = lax.all_to_all(mine, 'seq', 1, 0, tiled=True)  17.5 us
    dot_general x1, matrix products, per_device(): jnp.dot(lower, rising.reshape(tok_rows, modes * width), precision=lax.Pre...  13.9 us
  transfers between devices with their start and end apart: 4, of which 3 were waited for; matrix products, arithmetic and copies ran while one was open for 0% of the time, Pallas kernels for 0%

commit v1 on v0

--- a/solution.py
+++ b/solution.py
@@ -4,6 +4,23 @@
 from jax.sharding import PartitionSpec as P
 
 TAPS = 3
+
+
+def shelves_handle(obj, in_array):
+    group_axis = "ch"
+    heard = lax.psum(1, group_axis)
+    val = lax.axis_index(group_axis)
+    a_next, oldest, top = (heard, val, obj.shape[1])
+    xs_all = []
+    for to_i in [*range(a_next)]:
+        xs_all.append((to_i, (to_i + 1) % a_next))
+    v_next, response = (obj, None)
+    for j0 in tuple(range(a_next)):
+        f_now = lax.ppermute(v_next, group_axis, xs_all) if j0 < a_next - 1 else None
+        state_next = in_array(v_next, (oldest - j0) % a_next * top)
+        response = state_next if response is None else response + state_next
+        v_next = f_now
+    return response
 
 
 def passed_along(block, axis, distance):
@@ -39,8 +56,15 @@
     mine = lax.dynamic_index_in_dim(features, lax.axis_index("ch"), 2, False)
     rows = lax.all_to_all(mine, "seq", 1, 0, tiled=True)
     rows = rows.reshape(n_seq * tok_rows, piece)
-    block = lax.all_gather(rows, "ch", axis=1, tiled=True)
-    partial = jnp.einsum("td,kdc->ktc", block, w_in, preferred_element_type=jnp.float32)
+    partial = shelves_handle(
+        rows,
+        lambda part_2, offset_2: jnp.einsum(
+            "td,kdc->ktc",
+            part_2,
+            lax.dynamic_slice_in_dim(w_in, offset_2, part_2.shape[1], axis=1),
+            preferred_element_type=jnp.float32,
+        ),
+    )
     return lax.psum_scatter(partial, "seq", scatter_dimension=1, tiled=True)
 
 

time: 416 us -> 472 us (1.13)
  matrix products: 32.8 us -> 95.2 us
  blocking collectives: 47.9 us -> 30.3 us
  waiting for transfers between devices: 288 us -> 271 us
  starting transfers between devices: 1.37 us -> 17.4 us
  local copies, waits for them, and re-layouts: 8.82 us -> 17.8 us
    dot_general x1 -> x8, matrix products: 18.9 us -> 81.3 us  [project(): jnp.einsum('td,kdc->ktc', part_2, lax.dynamic_slice_in_dim(w_in, offset_2...]
    all_gather x1 -> x0, waiting for transfers between devices: 37.4 us -> none  [project(): block = lax.all_gather(rows, 'ch', axis=1, tiled=True)]
    all_to_all x1 -> x0, blocking collectives: 17.5 us -> none  [project(): rows = lax.all_to_all(mine, 'seq', 1, 0, tiled=True)]
    all_to_all x0 -> x1, waiting for transfers between devices: none -> 12.5 us  [project(): rows = lax.all_to_all(mine, 'seq', 1, 0, tiled=True)]
    ppermute x0 -> x7, starting transfers between devices: none -> 11 us  [shelves_handle(): lax.ppermute(v_next, group_axis, xs_all)]
    reduce_sum x0 -> x2, local copies, waits for them, and re-layouts: none -> 5.09 us  [the longest x1 2.55 us: per_device(): local = jnp.sum(falling * prefix, axis=1)]
    all_to_all x0 -> x1, starting transfers between devices: none -> 5.09 us  [project(): rows = lax.all_to_all(mine, 'seq', 1, 0, tiled=True)]
  transfers between devices with their start and end apart: 4 -> 11, of which waited for: 3 -> 8; matrix products, arithmetic and copies ran while one was open for 0% -> 10% of each run, Pallas kernels for 0% -> 0%
where the time goes in v1:
time: 472 us; the launch traced here: 471 us
  waiting for transfers between devices  271 us (57%)
  matrix products  95.2 us (20%)
  blocking collectives  30.3 us (6%)
  other arithmetic  25.1 us (5%)
  local copies, waits for them, and re-layouts  17.8 us (4%)
  starting transfers between devices  17.4 us (4%)
  between operations  13.6 us (3%)
    reduce_scatter x1, waiting for transfers between devices, project(): return lax.psum_scatter(partial, 'seq', scatter_dimension=1, tiled=True)  215 us
    dot_general x8, matrix products, project(): jnp.einsum('td,kdc->ktc', part_2, lax.dynamic_slice_in_dim(w_in, offset_2...  81.3 us
    all_gather x1, waiting for transfers between devices, project(): features = lax.all_gather(inputs, 'ch', axis=1, tiled=True)  39.5 us
    all_gather x2, blocking collectives, carried_in(): gathered = jax.tree.map(lambda a: lax.all_gather(a, axis), part)  30.3 us
    dot_general x1, matrix products, per_device(): jnp.dot(lower, rising.reshape(tok_rows, modes * width), precision=lax.Pre...  13.9 us
    all_to_all x1, waiting for transfers between devices, project(): rows = lax.all_to_all(mine, 'seq', 1, 0, tiled=True)  12.5 us
    ppermute x7, starting transfers between devices, shelves_handle(): lax.ppermute(v_next, group_axis, xs_all)  11 us
  transfers between devices with their start and end apart: 11, of which 8 were waited for; matrix products, arithmetic and copies ran while one was open for 10% of the time, Pallas kernels for 0%

profile of v1, /device:TPU:26, one launch (start us, length us, event | category | flops | bytes accessed | tf_op | source)
XLA Modules:
  0.0 470.8 jit_solution(15886026251056045584)
XLA Ops:
  6.5 0.7 all-gather.4.cloned.1.call-update
  7.3 39.5 %all-gather.4.cloned.1.call-done = bf16[256,8192]{1,0:T(8,128)(2,1)} async-done(((bf16[256,1024]{1,0:T(8,128)(2,1)}), bf16[256,8192]{1,0:T(8,128)(2,1)}) %all-gather.4.cloned.1.call-update) | async-done | bytes 4194320 | tf_op jit(solution)/shard_map/all_gather | solution.py:53
  46.8 3.6 copy.58
  50.4 1.1 constant_dynamic-slice_fusion
  51.5 1.0 copy.64
  52.4 5.1 %all-to-all-start = ((bf16[256,4,256]{2,0,1:T(8,128)(2,1)}), bf16[256,4,256]{2,0,1:T(8,128)(2,1)S(1)}, u32[]{:S(2)}, u32[]{:S(2)}) async-start(bf16[256,4,256]{2,0,1:T(8,128)(2,1)} %bitcast.71), calls=%async_computation | async-start | bytes 1048576 | tf_op jit(solution)/shard_map/all_to_all | solution.py:57
  57.5 12.5 %all-to-all-done = bf16[256,4,256]{2,0,1:T(8,128)(2,1)S(1)} async-done(((bf16[256,4,256]{2,0,1:T(8,128)(2,1)}), bf16[256,4,256]{2,0,1:T(8,128)(2,1)S(1)}, u32[]{:S(2)}, u32[]{:S(2)}) %all-to-all-start) | async-done | bytes 524320 | tf_op jit(solution)/shard_map/all_to_all | solution.py:57
  70.1 7.9 %fusion.15 = f32[3,1024,1024]{2,1,0:T(8,128)} fusion(bf16[1024,256,1]{1,0,2:T(8,128)(2,1)S(1)} %bitcast.83, bf16[3,2048,1024]{2,1,0:T(8,128)(2,1)} %param.9, s32[]{:T(128)S(6)} %select_n.70), kind=kOutput, calls=%fused_computation.26 | convolution fusion | flops 1610612736 | bytes 14680068 | tf_op jit(solution)/shard_map/td,kdc->ktc/dot_general | solution.py:61
  78.0 0.7 collective-permute-done
  78.7 0.7 collective-permute-start.1
  79.4 7.7 %fusion.13 = f32[3,1024,1024]{2,1,0:T(8,128)} fusion(bf16[3,2048,1024]{2,1,0:T(8,128)(2,1)} %param.9, s32[]{:T(128)S(6)} %select_n.73, bf16[1024,256]{1,0:T(8,128)(2,1)S(1)} %collective-permute-done), kind=kOutput, calls=%fused_computation.24 | convolution fusion | flops 1610612736 | bytes 14680068 | tf_op jit(solution)/shard_map/td,kdc->ktc/dot_general | solution.py:61
  87.3 1.5 collective-permute-start.2
  88.8 6.3 %fusion.11 = f32[3,1024,1024]{2,1,0:T(8,128)} fusion(bf16[3,2048,1024]{2,1,0:T(8,128)(2,1)S(1)} %bitcast.79, s32[]{:T(128)S(6)} %select_n.75, bf16[1024,256]{1,0:T(8,128)(2,1)S(1)} %collective-permute-done.1), kind=kOutput, calls=%fused_computation.22 | convolution fusion | flops 1610612736 | bytes 14680068 | tf_op jit(solution)/shard_map/td,kdc->ktc/dot_general | solution.py:61
  95.1 0.8 collective-permute-done.2
  95.9 1.0 collective-permute-start.3
  96.9 6.5 %fusion.9 = f32[3,1024,1024]{2,1,0:T(8,128)} fusion(bf16[3,2048,1024]{2,1,0:T(8,128)(2,1)S(1)} %bitcast.79, s32[]{:T(128)S(6)} %select_n.77, bf16[1024,256]{1,0:T(8,128)(2,1)S(1)} %collective-permute-done.2), kind=kOutput, calls=%fused_computation.20 | convolution fusion | flops 1610612736 | bytes 14680068 | tf_op jit(solution)/shard_map/td,kdc->ktc/dot_general | solution.py:61
  103.3 1.2 collective-permute-done.3
  104.5 2.0 collective-permute-start.4
  106.5 6.3 %fusion.7 = f32[3,1024,1024]{2,1,0:T(8,128)} fusion(bf16[3,2048,1024]{2,1,0:T(8,128)(2,1)S(1)} %bitcast.79, s32[]{:T(128)S(6)} %select_n.79, bf16[1024,256]{1,0:T(8,128)(2,1)S(1)} %collective-permute-done.3), kind=kOutput, calls=%fused_computation.18 | convolution fusion | flops 1610612736 | bytes 14680068 | tf_op jit(solution)/shard_map/td,kdc->ktc/dot_general | solution.py:61
  113.1 2.8 collective-permute-start.5
  115.9 6.4 %fusion.5 = f32[3,1024,1024]{2,1,0:T(8,128)} fusion(bf16[3,2048,1024]{2,1,0:T(8,128)(2,1)S(1)} %bitcast.79, s32[]{:T(128)S(6)} %select_n.81, bf16[1024,256]{1,0:T(8,128)(2,1)S(1)} %collective-permute-done.4), kind=kOutput, calls=%fused_computation.16 | convolution fusion | flops 1610612736 | bytes 14680068 | tf_op jit(solution)/shard_map/td,kdc->ktc/dot_general | solution.py:61
  122.3 3.2 collective-permute-start.6
  125.4 6.4 %fusion.3 = f32[3,1024,1024]{2,1,0:T(8,128)} fusion(bf16[3,2048,1024]{2,1,0:T(8,128)(2,1)S(1)} %bitcast.79, s32[]{:T(128)S(6)} %select_n.83, bf16[1024,256]{1,0:T(8,128)(2,1)S(1)} %collective-permute-done.5), kind=kOutput, calls=%fused_computation.14 | convolution fusion | flops 1610612736 | bytes 14680068 | tf_op jit(solution)/shard_map/td,kdc->ktc/dot_general | solution.py:61
  131.8 33.7 %add_bitcast_fusion = f32[3,1024,1024]{1,2,0:T(8,128)} fusion(f32[3,1024,1024]{2,1,0:T(8,128)} %fusion.3, f32[3,1024,1024]{2,1,0:T(8,128)} %fusion.5, f32[3,1024,1024]{2,1,0:T(8,128)} %fusion.7, f32[3,1024,1024]{2,1,0:T(8,128)} %fusion.9, f32[3,1024,1024]{2,1,0:T(8,128)} %fusion.11, f32[3,1024,1024]{2,1,0:T(8,128)} %fusion.15, f32[3,1024,1024]{2,1,0:T(8,128)} %fusion.13, ...), kind=kOutput, calls=%fused_computation.6 | convolution fusion | flops 1632632832 | bytes 102760448 | tf_op jit(solution)/shard_map/td,kdc->ktc/dot_general | solution.py:61
  165.6 0.7 copy-done.3
  166.4 0.6 fusion.38
  167.0 215.2 %reduce-scatter.2.cloned.1.call-done = f32[3,256,1024]{1,2,0:T(8,128)} async-done(((f32[3,1024,1024]{1,2,0:T(8,128)}), f32[3,256,1024]{1,2,0:T(8,128)}) %reduce-scatter.2.cloned.1.call-update) | async-done | bytes 3145744 | tf_op jit(solution)/shard_map/reduce_scatter | solution.py:68
  382.2 2.0 convert_element_type.10
  384.8 1.3 collective-permute-start.7
  386.1 15.7 %all-gather = f32[64,1024]{1,0:T(8,128)S(1)} all-gather(f32[16,1024]{1,0:T(8,128)S(1)} %get-tuple-element.63), channel_id=2, replica_groups=mesh['seq'=4,'ch'=8] {'seq'}, dimensions={0}, use_global_device_ids=true | all-gather | bytes 327680 | tf_op jit(solution)/shard_map/all_gather | solution.py:34
  401.9 0.6 copy.59
  403.0 1.0 maximum_convert_fusion
  403.9 3.2 fusion
  407.1 1.1 fusion.17
  408.2 2.5 copy.41
  410.8 4.1 multiply_reduce_fusion.1
  414.9 14.6 %all-gather.1 = f32[64,1024]{1,0:T(8,128)} all-gather(f32[16,1024]{1,0:T(8,128)S(1)} %multiply_reduce_fusion.1), channel_id=3, replica_groups=mesh['seq'=4,'ch'=8] {'seq'}, dimensions={0}, use_global_device_ids=true | all-gather | bytes 327680 | tf_op jit(solution)/shard_map/all_gather | solution.py:34
  429.5 2.9 while.12
  429.5 0.9 bitcast_add_fusion.2
  430.4 0.9 bitcast_add_fusion.2
  431.3 0.9 bitcast_add_fusion.2
  432.4 3.9 bitcast_multiply_fusion.1
  436.5 13.9 %multiply_reduce_fusion.2 = f32[256,1024]{1,0:T(8,128)} fusion(f32[16,1024,256]{2,1,0:T(8,128)S(1)} %bitcast.77, f32[16,1024]{1,0:T(8,128)S(1)} %get-tuple-element.61, f32[256]{0:T(256)S(1)} %iota_add_fusion.1, f32[16,1024]{1,0:T(8,128)S(1)} %copy-done.2), kind=kOutput, calls=%fused_computation.5 | convolution fusion | flops 12901482496 | bytes 17957888 | tf_op jit(solution)/shard_map/dot_general | solution.py:100
  450.4 2.6 copy.43
  453.0 3.8 multiply_reduce_fusion
  456.7 2.5 copy.44
  459.3 2.6 fusion.19
  461.9 2.0 copy.45
  (36 shorter events, 1.6 us)
Async XLA Ops:
  6.5 40.3 %all-gather.4.cloned.1.call-start = ((), (), s32[]{:S(2)}) async-start(), calls=%async_computation.2 | async-start | bytes 4718592 | tf_op jit(solution)/shard_map/all_gather | solution.py:53
  52.4 17.6 %all-to-all-start = ((bf16[256,4,256]{2,0,1:T(8,128)(2,1)}), bf16[256,4,256]{2,0,1:T(8,128)(2,1)S(1)}, u32[]{:S(2)}, u32[]{:S(2)}) async-start(bf16[256,4,256]{2,0,1:T(8,128)(2,1)} %bitcast.71), calls=%async_computation | async-start | bytes 1048576 | tf_op jit(solution)/shard_map/all_to_all | solution.py:57
  57.5 324.7 %reduce-scatter.2.cloned.1.call-start = ((), (), s32[]{:S(2)}) async-start(), calls=%async_computation.3 | async-start | bytes 15728640 | tf_op jit(solution)/shard_map/reduce_scatter | solution.py:68
  70.1 8.6 %collective-permute-start = (bf16[1024,256]{1,0:T(8,128)(2,1)S(1)}, bf16[1024,256]{1,0:T(8,128)(2,1)S(1)}, u32[]{:S(2)}, u32[]{:S(2)}) collective-permute-start(bf16[1024,256]{1,0:T(8,128)(2,1)S(1)} %bitcast.82), channel_id=1, source_target_pairs={{0,1},{1,2},{2,3},{3,4},{4,5},{5,6},{6,7},{7,0},{8,9},{9,10},{10,1... | collective-permute-start | bytes 1572872 | tf_op jit(solution)/shard_map/ppermute | solution.py:19
  70.1 18.7 %slice-start = ((s8[12582912]{0:T(1024)(128)(4,1)}), s8[4194304]{0:T(1024)(128)(4,1)S(1)}, s32[]{:S(2)}) async-start(s8[12582912]{0:T(1024)(128)(4,1)} %bitcast.78), calls=%async_computation.4 | async-start | bytes 8388608
  70.1 18.7 %slice-start.1 = ((s8[12582912]{0:T(1024)(128)(4,1)}), s8[4194304]{0:T(1024)(128)(4,1)S(1)}, s32[]{:S(2)}) async-start(s8[12582912]{0:T(1024)(128)(4,1)} %bitcast.78), calls=%async_computation.5 | async-start | bytes 8388608
  78.0 10.8 %slice-start.2 = ((s8[12582912]{0:T(1024)(128)(4,1)}), s8[4194304]{0:T(1024)(128)(4,1)S(1)}, s32[]{:S(2)}) async-start(s8[12582912]{0:T(1024)(128)(4,1)} %bitcast.78), calls=%async_computation.6 | async-start | bytes 8388608
  78.7 8.6 %collective-permute-start.1 = (bf16[1024,256]{1,0:T(8,128)(2,1)S(1)}, bf16[1024,256]{1,0:T(8,128)(2,1)S(1)}, u32[]{:S(2)}, u32[]{:S(2)}) collective-permute-start(bf16[1024,256]{1,0:T(8,128)(2,1)S(1)} %collective-permute-done), channel_id=1, source_target_pairs={{0,1},{1,2},{2,3},{3,4},{4,5},{5,6},{6,7},{7,0},{8,9},{9,10},{10,1... | collective-permute-start | bytes 1572872 | tf_op jit(solution)/shard_map/ppermute | solution.py:19
  87.3 8.6 %collective-permute-start.2 = (bf16[1024,256]{1,0:T(8,128)(2,1)S(1)}, bf16[1024,256]{1,0:T(8,128)(2,1)S(1)}, u32[]{:S(2)}, u32[]{:S(2)}) collective-permute-start(bf16[1024,256]{1,0:T(8,128)(2,1)S(1)} %collective-permute-done.1), channel_id=1, source_target_pairs={{0,1},{1,2},{2,3},{3,4},{4,5},{5,6},{6,7},{7,0},{8,9},{9,10},{10,1... | collective-permute-start | bytes 1572872 | tf_op jit(solution)/shard_map/ppermute | solution.py:19
  95.9 8.6 %collective-permute-start.3 = (bf16[1024,256]{1,0:T(8,128)(2,1)S(1)}, bf16[1024,256]{1,0:T(8,128)(2,1)S(1)}, u32[]{:S(2)}, u32[]{:S(2)}) collective-permute-start(bf16[1024,256]{1,0:T(8,128)(2,1)S(1)} %collective-permute-done.2), channel_id=1, source_target_pairs={{0,1},{1,2},{2,3},{3,4},{4,5},{5,6},{6,7},{7,0},{8,9},{9,10},{10,1... | collective-permute-start | bytes 1572872 | tf_op jit(solution)/shard_map/ppermute | solution.py:19
  104.5 8.6 %collective-permute-start.4 = (bf16[1024,256]{1,0:T(8,128)(2,1)S(1)}, bf16[1024,256]{1,0:T(8,128)(2,1)S(1)}, u32[]{:S(2)}, u32[]{:S(2)}) collective-permute-start(bf16[1024,256]{1,0:T(8,128)(2,1)S(1)} %collective-permute-done.3), channel_id=1, source_target_pairs={{0,1},{1,2},{2,3},{3,4},{4,5},{5,6},{6,7},{7,0},{8,9},{9,10},{10,1... | collective-permute-start | bytes 1572872 | tf_op jit(solution)/shard_map/ppermute | solution.py:19
  113.1 9.2 %collective-permute-start.5 = (bf16[1024,256]{1,0:T(8,128)(2,1)S(1)}, bf16[1024,256]{1,0:T(8,128)(2,1)S(1)}, u32[]{:S(2)}, u32[]{:S(2)}) collective-permute-start(bf16[1024,256]{1,0:T(8,128)(2,1)S(1)} %collective-permute-done.4), channel_id=1, source_target_pairs={{0,1},{1,2},{2,3},{3,4},{4,5},{5,6},{6,7},{7,0},{8,9},{9,10},{10,1... | collective-permute-start | bytes 1572872 | tf_op jit(solution)/shard_map/ppermute | solution.py:19
  122.3 9.6 %collective-permute-start.6 = (bf16[1024,256]{1,0:T(8,128)(2,1)S(1)}, bf16[1024,256]{1,0:T(8,128)(2,1)S(1)}, u32[]{:S(2)}, u32[]{:S(2)}) collective-permute-start(bf16[1024,256]{1,0:T(8,128)(2,1)S(1)} %collective-permute-done.5), channel_id=1, source_target_pairs={{0,1},{1,2},{2,3},{3,4},{4,5},{5,6},{6,7},{7,0},{8,9},{9,10},{10,1... | collective-permute-start | bytes 1572872 | tf_op jit(solution)/shard_map/ppermute | solution.py:19
  165.5 0.8 copy-start.3
  165.5 0.9 copy-start
  384.8 17.7 %collective-permute-start.7 = (bf16[3,2,1024]{2,1,0:T(2,128)(2,1)S(1)}, bf16[3,2,1024]{2,1,0:T(2,128)(2,1)S(1)}, u32[]{:S(2)}, u32[]{:S(2)}) collective-permute-start(bf16[3,2,1024]{2,1,0:T(2,128)(2,1)S(1)} %copy.39), channel_id=1, source_target_pairs={{0,8},{8,16},{16,24},{1,9},{9,17},{17,25},{2,10},{10,18},{18,26},{... | collective-permute-start | bytes 36872 | tf_op jit(solution)/shard_map/ppermute | solution.py:29
  432.4 4.0 copy-start.1
  432.4 4.0 copy-start.2
  436.4 22.8 %copy-start.4 = (f32[1024]{0:T(1024)S(1)}, f32[1024]{0:T(1024)}, u32[]{:S(2)}) copy-start(f32[1024]{0:T(1024)} %param.13) | copy-start | bytes 12292
Sparse Core Ops, SparseCore 0:
  9.2 37.5 all-gather.3
  165.7 216.5 reduce-scatter.1
